TPU v7x, 512 devices: a whole 4x4x16 slice. The times are simulated.
512 devices in a mesh: row: 16 (over z), col: 32 (over y, x, core).
Axes of the slice: x: 4, y: 4, z: 16, core: 2. Of those that a mesh axis runs over, the one named last changes fastest.
Arguments:
- node_feats: bfloat16 [262144, 512], P(('row', 'col')), may hold values from -8 to 8
- source_feats: bfloat16 [4096, 512], P('col'), may hold values from -6 to 6
- nbr_blocks: int32 [2048, 8], P(('row', 'col')), may hold values from 0 to 31
- nbr_count: int32 [2048], P(('row', 'col')), may hold values from 1 to 8
- adj_tiles: bfloat16 [2048, 8, 128, 128], P(('row', 'col')), may hold values from -0.1875 to 0.1875
- pos_index: int32 [262144], P(('row', 'col')), may hold values from 0 to 511
- noise_block_rows: int32 [16], replicated, may hold values from 0 to 15
- w_self: bfloat16 [512, 512], replicated, may hold values from -0.25 to 0.25
- w_neigh: bfloat16 [512, 512], replicated, may hold values from -0.25 to 0.25
Outputs:
- grad_self: float32 [512, 512], replicated
- neighbour_weight_gradient: float32 [512, 512], replicated
- loss: float32 [], replicated
All inputs are finite; a program needn't handle non-finite values.
Results may differ from a plain program's by a relative error of at most 0.002.
Values may be sent and summed in bfloat16 or wider, within the bound.
No kernel may reach another device: no remote copies, remote signals or barrier semaphores. Data moves between devices by JAX's collectives and lax.ppermute only.
A program may use at most 64 MiB of HBM per device.

v0:
```python
import jax
import jax.numpy as jnp
from jax import lax
from jax.sharding import PartitionSpec as P

BLOCK = 128
NOISE = 128
softness_divisor = 0.2


def embed(pre):
    return pre * lax.rsqrt(jnp.sum(pre * pre, axis=-1, keepdims=True) + 1e-06)


def body(
    node_feats,
    source_feats,
    nbr_blocks,
    nbr_count,
    adj_tiles,
    pos_index,
    noise_block_rows,
    w_self,
    w_neigh,
):
    rows = node_feats.shape[0]
    width = node_feats.shape[1]
    slots = adj_tiles.shape[1]
    highest = lax.Precision.HIGHEST
    nodes = rows * lax.axis_size("row") * lax.axis_size("col")
    scale_factor = 1.0 / softness_divisor
    valid = jnp.arange(slots, dtype=jnp.int32)[None, :] < nbr_count[:, None]
    tiles = adj_tiles * valid[:, :, None, None].astype(jnp.bfloat16)
    piece = lax.all_gather(source_feats, "col", axis=0, tiled=True)
    count = piece.shape[0] // BLOCK
    blocks = piece.reshape(count, BLOCK, width)
    indicator_matrix = (
        nbr_blocks[:, :, None] == jnp.arange(count, dtype=jnp.int32)[None, None, :]
    ).astype(jnp.bfloat16)
    selected = jnp.einsum(
        "bkc,cjd->bkjd", indicator_matrix, blocks, preferred_element_type=jnp.float32
    ).astype(jnp.bfloat16)
    summed = jnp.einsum("bkij,bkjd->bid", tiles, selected, preferred_element_type=jnp.float32)
    agg = summed.reshape(rows, width).astype(jnp.bfloat16)
    pre = jnp.dot(node_feats, w_self, preferred_element_type=jnp.float32) + jnp.dot(
        agg, w_neigh, preferred_element_type=jnp.float32
    )
    emb32, pull = jax.vjp(embed, pre)
    zeta_bf = emb32.astype(jnp.bfloat16)
    candidates = lax.all_gather(zeta_bf[:NOISE], "row", axis=0, tiled=True)
    my_row = lax.axis_index("row")
    my_noise = noise_block_rows[my_row]
    noise_emb = lax.dynamic_slice_in_dim(candidates, my_noise * NOISE, NOISE, 0).astype(jnp.float32)
    zeta = zeta_bf.astype(jnp.float32)
    pairing = (pos_index[:, None] == jnp.arange(rows, dtype=jnp.int32)[None, :]).astype(jnp.float32)
    partner = jnp.dot(pairing, zeta, precision=highest)
    s_pos = jnp.sum(zeta * partner, axis=-1) * scale_factor
    s_neg = jnp.dot(zeta, noise_emb.T, precision=highest) * scale_factor
    loss_part = (jnp.sum(jax.nn.softplus(-s_pos)) + jnp.sum(jax.nn.softplus(s_neg)) / NOISE) / nodes
    grad_pos = -jax.nn.sigmoid(-s_pos) / nodes
    grad_neg = jax.nn.sigmoid(s_neg) / (NOISE * nodes)
    anchor = scale_factor * (
        grad_pos[:, None] * partner + jnp.dot(grad_neg, noise_emb, precision=highest)
    )
    partner_grad = jnp.dot(pairing.T, scale_factor * grad_pos[:, None] * zeta, precision=highest)
    dnoise = scale_factor * jnp.dot(grad_neg.T, zeta, precision=highest)
    groups = lax.axis_size("row")
    collected = lax.all_gather(dnoise.astype(jnp.bfloat16), "row", axis=0, tiled=True)
    owned = (noise_block_rows == my_row).astype(jnp.float32)
    returned = jnp.dot(
        owned[None, :],
        collected.astype(jnp.float32).reshape(groups, NOISE * width),
        precision=highest,
    )
    returned = returned.reshape(NOISE, width)
    dzeta = anchor + partner_grad
    dzeta = dzeta.at[:NOISE].add(returned)
    gpre = pull(dzeta)[0].astype(jnp.bfloat16)
    part_self = jnp.dot(node_feats.T, gpre, preferred_element_type=jnp.float32)
    neighbour_partial = jnp.dot(agg.T, gpre, preferred_element_type=jnp.float32)
    grad_self, neighbour_weight_gradient, loss = lax.psum(
        (part_self, neighbour_partial, loss_part), ("row", "col")
    )
    return (grad_self, neighbour_weight_gradient, loss)


def solution(mesh):
    in_specs = (
        P(("row", "col"), None),
        P("col", None),
        P(("row", "col"), None),
        P(("row", "col")),
        P(("row", "col"), None, None, None),
        P(("row", "col")),
        P(),
        P(),
        P(),
    )
    out_specs = (P(), P(), P())
    return jax.shard_map(body, mesh=mesh, in_specs=in_specs, out_specs=out_specs, check_vma=False)
```

profile of v0, /device:TPU:1, one launch (start us, length us, event | category | flops | bytes accessed | tf_op | source)
XLA Modules:
  0.0 734.0 jit_solution(15400814606287364603)
XLA Ops:
  7.2 0.7 all-gather.4.cloned.1.call-update
  8.0 0.7 fusion.26
  8.7 1.5 fusion.36
  10.2 68.1 %all-gather.4.cloned.1.call-done = bf16[4096,512]{1,0:T(8,128)(2,1)} async-done(((bf16[128,512]{1,0:T(8,128)(2,1)}), bf16[4096,512]{1,0:T(8,128)(2,1)}) %all-gather.4.cloned.1.call-update) | async-done | bytes 4194320 | tf_op jit(solution)/shard_map/all_gather | solution.py:34
  78.3 5.6 fusion.1
  83.9 2.6 fusion.8
  87.4 0.7 slice.24
  88.2 0.6 dynamic_slice.6
  89.4 66.7 %all-gather.6.cloned.1.call-done = bf16[2048,512]{0,1:T(8,128)(2,1)} async-done(((bf16[128,512]{0,1:T(8,128)(2,1)}), bf16[2048,512]{0,1:T(8,128)(2,1)}) %all-gather.6.cloned.1.call-update) | async-done | bytes 2097168 | tf_op jit(solution)/shard_map/all_gather | solution.py:50
  156.1 1.9 fusion.18
  158.0 1.4 fusion.9
  159.7 0.6 fusion.10
  160.3 0.6 fusion.25
  160.9 1.6 fusion.7
  162.5 1.2 convolution_add_fusion.1
  163.7 66.2 %all-gather.8.cloned.1.call-done = bf16[2048,512]{1,0:T(8,128)(2,1)} async-done(((bf16[128,512]{1,0:T(8,128)(2,1)}), bf16[2048,512]{1,0:T(8,128)(2,1)}) %all-gather.8.cloned.1.call-update) | async-done | bytes 2097168 | tf_op jit(solution)/shard_map/all_gather | solution.py:68
  229.9 3.2 reshape.99
  233.1 2.0 fusion.3
  235.9 2.5 fusion.37
  238.4 1.4 convolution_bitcast_fusion
  241.1 110.9 %psum.23 = f32[]{:T(128)} all-reduce(f32[]{:T(128)S(6)} %div.45), channel_id=1, replica_groups=mesh['row'=16,'col'=32] {'row','col'}, use_global_device_ids=true, to_apply=%region_7.8 | all-reduce | flops 1 | bytes 8 | tf_op jit(solution)/shard_map/psum | solution.py:81
  351.9 370.7 %all-reduce.3.cloned.1.call-done = (f32[512,512]{0,1:T(8,128)}, f32[512,512]{1,0:T(8,128)}) async-done(((f32[512,512]{0,1:T(8,128)}, f32[512,512]{1,0:T(8,128)}), (f32[512,512]{0,1:T(8,128)}, f32[512,512]{1,0:T(8,128)})) %all-reduce.3.cloned.1.call-update) | async-done | bytes 2097168 | tf_op jit(solution)/shard_map/psum | solution.py:81
  722.6 2.5 copy.12
  725.2 2.3 copy.35
  (27 shorter events, 2.1 us)
Async XLA Ops:
  7.2 1.5 copy-start
  7.2 71.1 %all-gather.4.cloned.1.call-start = ((), (), s32[]{:S(2)}) async-start(), calls=%async_computation | async-start | bytes 4325376 | tf_op jit(solution)/shard_map/all_gather | solution.py:34
  7.9 148.2 %all-gather.6.cloned.1.call-start = ((), (), s32[]{:S(2)}) async-start(), calls=%async_computation.1 | async-start | bytes 2228224 | tf_op jit(solution)/shard_map/all_gather | solution.py:50
  78.3 5.6 copy-start.5
  83.8 2.7 copy-start.2
  86.5 0.8 copy-start.1
  86.5 1.7 copy-start.4
  86.5 73.1 %copy-start.3 = (s32[512]{0:T(512)S(1)}, s32[512]{0:T(512)}, u32[]{:S(2)}) copy-start(s32[512]{0:T(512)} %param.16) | copy-start | bytes 6148
  88.1 141.8 %all-gather.8.cloned.1.call-start = ((), (), s32[]{:S(2)}) async-start(), calls=%async_computation.2 | async-start | bytes 2228224 | tf_op jit(solution)/shard_map/all_gather | solution.py:68
  159.4 563.2 %all-reduce.3.cloned.1.call-start = ((), (), s32[]{:S(2)}) async-start(), calls=%async_computation.3 | async-start | bytes 4194304 | tf_op jit(solution)/shard_map/psum | solution.py:81
Sparse Core Ops, SparseCore 0:
  11.1 67.0 all-gather.3
  88.2 67.8 all-gather.5
  159.5 70.3 all-gather.7
  240.0 482.5 all-reduce.2
where the time goes:
time: 734 us
  waiting for transfers between devices  572 us (78%)
  blocking collectives  111 us (15%)
  matrix products  22.8 us (3%)
  between operations  15.8 us (2%)
  local copies, waits for them, and re-layouts  9.65 us (1%)
    psum x1, waiting for transfers between devices, body(): lax.psum((part_self, neighbour_partial, loss_part), ('row', 'col'))  371 us
    psum x1, blocking collectives, body(): lax.psum((part_self, neighbour_partial, loss_part), ('row', 'col'))  111 us
    all_gather x1, waiting for transfers between devices, body(): piece = lax.all_gather(source_feats, 'col', axis=0, tiled=True)  68.1 us
    all_gather x1, waiting for transfers between devices, body(): candidates = lax.all_gather(zeta_bf[:NOISE], 'row', axis=0, tiled=True)  66.7 us
    all_gather x1, waiting for transfers between devices, body(): lax.all_gather(dnoise.astype(jnp.bfloat16), 'row', axis=0, tiled=True)  66.2 us
  transfers between devices with their start and end apart: 4, of which 4 were waited for; matrix products, arithmetic and copies ran while one was open for 1% of the time, Pallas kernels for 0%

commit v1 on v0

--- a/solution.py
+++ b/solution.py
@@ -79,7 +79,7 @@
     part_self = jnp.dot(node_feats.T, gpre, preferred_element_type=jnp.float32)
     neighbour_partial = jnp.dot(agg.T, gpre, preferred_element_type=jnp.float32)
     grad_self, neighbour_weight_gradient, loss = lax.psum(
-        (part_self, neighbour_partial, loss_part), ("row", "col")
+        lax.psum((part_self, neighbour_partial, loss_part), "col"), "row"
     )
     return (grad_self, neighbour_weight_gradient, loss)
 

time: 734 us -> 542 us (0.74); the launches traced: 734 us -> 533 us
  waiting for transfers between devices: 572 us -> 394 us
  blocking collectives: 111 us -> 88.7 us
    psum x1 -> x2, waiting for transfers between devices: 371 us -> 192 us  [the longest x1 144 us: body(): lax.psum((part_self, neighbour_partial, loss_part), 'col')]
    psum x1 -> x2, blocking collectives: 111 us -> 88.7 us  [the longest x1 63.4 us: body(): lax.psum((part_self, neighbour_partial, loss_part), 'col')]
  transfers between devices with their start and end apart: 4 -> 5, of which waited for: 4 -> 5; matrix products, arithmetic and copies ran while one was open for 1% -> 1% of each run, Pallas kernels for 0% -> 0%
where the time goes in v1:
time: 542 us; the launch traced here: 533 us
  waiting for transfers between devices  394 us (73%)
  blocking collectives  88.7 us (16%)
  matrix products  22.8 us (4%)
  between operations  15.8 us (3%)
  local copies, waits for them, and re-layouts  9.66 us (2%)
    psum x1, waiting for transfers between devices, body(): lax.psum((part_self, neighbour_partial, loss_part), 'col')  144 us
    all_gather x1, waiting for transfers between devices, body(): piece = lax.all_gather(source_feats, 'col', axis=0, tiled=True)  68.1 us
    all_gather x1, waiting for transfers between devices, body(): candidates = lax.all_gather(zeta_bf[:NOISE], 'row', axis=0, tiled=True)  66.7 us
    all_gather x1, waiting for transfers between devices, body(): lax.all_gather(dnoise.astype(jnp.bfloat16), 'row', axis=0, tiled=True)  66.2 us
    psum x1, blocking collectives, body(): lax.psum((part_self, neighbour_partial, loss_part), 'col')  63.4 us
    psum x1, waiting for transfers between devices, body(): lax.psum(lax.psum((part_self, neighbour_partial, loss_part), 'col'), 'row')  47.9 us
    psum x1, blocking collectives, body(): lax.psum(lax.psum((part_self, neighbour_partial, loss_part), 'col'), 'row')  25.3 us
  transfers between devices with their start and end apart: 5, of which 5 were waited for; matrix products, arithmetic and copies ran while one was open for 1% of the time, Pallas kernels for 0%

profile of v1, /device:TPU:1, one launch (start us, length us, event | category | flops | bytes accessed | tf_op | source)
XLA Modules:
  0.0 533.2 jit_solution(3668671691526717942)
XLA Ops:
  7.2 0.7 all-gather.4.cloned.1.call-update
  8.0 0.7 fusion.26
  8.7 1.5 fusion.36
  10.2 68.1 %all-gather.4.cloned.1.call-done = bf16[4096,512]{1,0:T(8,128)(2,1)} async-done(((bf16[128,512]{1,0:T(8,128)(2,1)}), bf16[4096,512]{1,0:T(8,128)(2,1)}) %all-gather.4.cloned.1.call-update) | async-done | bytes 4194320 | tf_op jit(solution)/shard_map/all_gather | solution.py:34
  78.3 5.6 %fusion.1 = bf16[4,8,128,512]{3,1,2,0:T(8,128)(2,1)S(1)} fusion(bf16[32,128,512,1]{2,1,0,3:T(8,128)(2,1)} %bitcast.39, s32[4,8]{1,0:T(4,128)} %param.13), kind=kOutput, calls=%fused_computation.2 | convolution fusion | flops 134218752 | bytes 8388736 | tf_op jit(solution)/shard_map/bkc,cjd->bkjd/dot_general | solution.py:40
  83.9 2.6 fusion.8
  87.4 0.7 slice.24
  89.4 66.7 %all-gather.6.cloned.1.call-done = bf16[2048,512]{0,1:T(8,128)(2,1)} async-done(((bf16[128,512]{0,1:T(8,128)(2,1)}), bf16[2048,512]{0,1:T(8,128)(2,1)}) %all-gather.6.cloned.1.call-update) | async-done | bytes 2097168 | tf_op jit(solution)/shard_map/all_gather | solution.py:50
  156.1 1.9 fusion.18
  158.0 1.4 fusion.9
  159.7 0.6 fusion.10
  160.9 1.6 fusion.7
  162.5 1.2 convolution_add_fusion.1
  163.7 66.2 %all-gather.8.cloned.1.call-done = bf16[2048,512]{1,0:T(8,128)(2,1)} async-done(((bf16[128,512]{1,0:T(8,128)(2,1)}), bf16[2048,512]{1,0:T(8,128)(2,1)}) %all-gather.8.cloned.1.call-update) | async-done | bytes 2097168 | tf_op jit(solution)/shard_map/all_gather | solution.py:68
  229.9 3.2 reshape.99
  233.1 2.0 fusion.3
  235.9 2.5 fusion.37
  238.4 1.4 convolution_bitcast_fusion
  239.9 144.2 %all-reduce.5.cloned.1.call-done = (f32[512,512]{0,1:T(8,128)}, f32[512,512]{1,0:T(8,128)}) async-done(((f32[512,512]{0,1:T(8,128)}, f32[512,512]{1,0:T(8,128)}), (f32[512,512]{0,1:T(8,128)}, f32[512,512]{1,0:T(8,128)})) %all-reduce.5.cloned.1.call-update) | async-done | bytes 2097168 | tf_op jit(solution)/shard_map/psum | solution.py:82
  385.4 63.4 %psum.46 = f32[]{:T(128)} all-reduce(f32[]{:T(128)S(6)} %div.45), channel_id=1, replica_groups=mesh['row'=16,'col'=32] {'col'}, use_global_device_ids=true, to_apply=%region_9.10 | all-reduce | flops 1 | bytes 8 | tf_op jit(solution)/shard_map/psum | solution.py:82
  448.7 25.3 %psum.47 = f32[]{:T(128)} all-reduce(f32[]{:T(128)} %psum.46), channel_id=1, replica_groups=mesh['row'=16,'col'=32] {'row'}, use_global_device_ids=true, to_apply=%region_10.11 | all-reduce | flops 1 | bytes 8 | tf_op jit(solution)/shard_map/psum | solution.py:81
  474.0 47.9 %all-reduce.7.cloned.1.call-done = (f32[512,512]{0,1:T(8,128)}, f32[512,512]{1,0:T(8,128)}) async-done(((f32[512,512]{0,1:T(8,128)}, f32[512,512]{1,0:T(8,128)}), (f32[512,512]{0,1:T(8,128)}, f32[512,512]{1,0:T(8,128)})) %all-reduce.7.cloned.1.call-update) | async-done | bytes 2097168 | tf_op jit(solution)/shard_map/psum | solution.py:81
  521.9 2.5 copy.12
  524.5 2.3 copy.37
  (31 shorter events, 3.3 us)
Async XLA Ops:
  7.2 1.5 copy-start
  7.2 71.1 %all-gather.4.cloned.1.call-start = ((), (), s32[]{:S(2)}) async-start(), calls=%async_computation | async-start | bytes 4325376 | tf_op jit(solution)/shard_map/all_gather | solution.py:34
  7.9 148.2 %all-gather.6.cloned.1.call-start = ((), (), s32[]{:S(2)}) async-start(), calls=%async_computation.1 | async-start | bytes 2228224 | tf_op jit(solution)/shard_map/all_gather | solution.py:50
  78.3 5.6 %copy-start.5 = (bf16[4,8,128,128]{3,2,1,0:T(8,128)(2,1)S(1)}, bf16[4,8,128,128]{3,2,1,0:T(8,128)(2,1)}, u32[]{:S(2)}) copy-start(bf16[4,8,128,128]{3,2,1,0:T(8,128)(2,1)} %param.15) | copy-start | bytes 3145732
  83.8 2.7 copy-start.2
  86.5 0.8 copy-start.1
  86.5 1.7 copy-start.4
  86.5 73.1 %copy-start.3 = (s32[512]{0:T(512)S(1)}, s32[512]{0:T(512)}, u32[]{:S(2)}) copy-start(s32[512]{0:T(512)} %param.16) | copy-start | bytes 6148
  88.1 141.8 %all-gather.8.cloned.1.call-start = ((), (), s32[]{:S(2)}) async-start(), calls=%async_computation.2 | async-start | bytes 2228224 | tf_op jit(solution)/shard_map/all_gather | solution.py:68
  159.4 224.7 %all-reduce.5.cloned.1.call-start = ((), (), s32[]{:S(2)}) async-start(), calls=%async_computation.3 | async-start | bytes 4194304 | tf_op jit(solution)/shard_map/psum | solution.py:82
  239.9 282.0 %all-reduce.7.cloned.1.call-start = ((), (), s32[]{:S(2)}) async-start(), calls=%async_computation.4 | async-start | bytes 4194304 | tf_op jit(solution)/shard_map/psum | solution.py:81
Sparse Core Ops, SparseCore 0:
  11.1 67.0 all-gather.3
  88.2 67.8 all-gather.5
  159.5 70.3 all-gather.7
  240.0 144.0 all-reduce.4
  386.4 135.5 all-reduce.6
